TPU v7x, 256 devices: a whole 4x4x8 slice. The times are simulated.
256 devices in a mesh: region: 8 (over z), row: 32 (over y, x, core).
Axes of the slice: x: 4, y: 4, z: 8, core: 2. Of those that a mesh axis runs over, the one named last changes fastest.
Arguments:
- state0: float32 [32, 131072], P(None, ('region', 'row')), may hold values from -6 to 6
- drive: bfloat16 [32, 131072], P(None, ('region', 'row')), may hold values from -6 to 6
- cotangent: float32 [32, 131072], P(None, ('region', 'row')), may hold values from -6 to 6
- excitatory: int32 [131072], P(('region', 'row')), may hold values 0 or 1
- tile_vals: bfloat16 [1024, 24, 128, 128], P(('region', 'row')), may hold values from 0.0039978027 to 0.039794922
- tile_cols: int32 [1024, 24], P(('region', 'row')), may hold values from 0 to 159
- tile_count: int32 [1024], P(('region', 'row')), may hold values from 1 to 24, as said below
- boundary_rows: int32 [8, 32, 8, 16], P('region', 'row'), may hold values from 0 to 511, as said below
- u_factor: bfloat16 [32, 131072], P(None, ('region', 'row')), may hold values from -1 to 1
- v_factor: bfloat16 [32, 131072], P(None, ('region', 'row')), may hold values from -0.015625 to 0.015625
Outputs:
- final_state: float32 [32, 131072], P(None, ('region', 'row'))
- grad_u: float32 [32, 131072], P(None, ('region', 'row'))
- grad_v: float32 [32, 131072], P(None, ('region', 'row'))
Inputs may be any that keep to these rules, and one draw needn't show every extreme that they name: tile_count[q] tiles of row tile q are live; its tiles j >= tile_count[q] take no part; the most, 24, is reached in every draw. `boundary_rows`: the 16 rows of one list are distinct. tile_cols[q, j] numbers a tile of 128 extended columns of the group of row tile q.
All inputs are finite; a program needn't handle non-finite values. No bound on the sum of `excitatory` on one device may be relied on, other than what follows from the above.
Results may differ from a plain program's by a relative error of at most 0.0055.
Values may be sent and summed in bfloat16 or wider, within the bound.
No kernel may reach another device: no remote copies, remote signals or barrier semaphores. Data moves between devices by JAX's collectives and lax.ppermute only.
A program may use at most 64 MiB of HBM per device.

v0:
```python
import jax
import jax.numpy as jnp
from jax import lax
from jax.sharding import Mesh
from jax.sharding import PartitionSpec as P

STEPS = 4
ROW = ("row_0", "row_1", "row_2")
REGION_ROW = ("region", "row_0", "row_1", "row_2")
leak = 0.5


def apply_tiles(ext_cols, flat_cols, live_tiles, flat_tiles, row_tiles):
    batch_rows, span_cols = ext_cols.shape
    blocks = ext_cols.reshape(batch_rows, span_cols // 128, 128)[:, flat_cols, :]
    blocks = jnp.where(live_tiles[None, :, None], blocks, jnp.zeros((), blocks.dtype))
    product = jnp.einsum("bsk,sik->bsi", blocks, flat_tiles, preferred_element_type=jnp.float32)
    summed = product.reshape(batch_rows, row_tiles, -1, 128).sum(axis=2)
    return summed.reshape(batch_rows, row_tiles * 128)


def from_each_region(x, me):
    everyone = lax.all_gather(x, "region", axis=0, tiled=False)
    mine = lax.dynamic_index_in_dim(everyone, me, axis=2, keepdims=False)
    return jnp.moveaxis(mine, 0, 1).reshape(x.shape[0], -1)


def local(
    state0,
    drive,
    cotangent,
    excitatory,
    tile_vals,
    tile_cols,
    tile_count,
    boundary_rows,
    u_factor,
    v_factor,
):
    lanes = lax.axis_size(ROW)
    groups = lax.axis_size("region")
    me = lax.axis_index("region")
    own_rows = state0.shape[1]
    own_tiles = own_rows // 128
    row_tiles = tile_vals.shape[0]
    chosen = boundary_rows.reshape(-1)
    bound_cols = chosen.shape[0]
    bound_tiles = bound_cols // 128
    per_lane = own_tiles + bound_tiles
    lane_of = tile_cols // per_lane
    at_lane = tile_cols % per_lane
    remapped = jnp.where(
        at_lane < own_tiles,
        lane_of * own_tiles + at_lane,
        lanes * own_tiles + lane_of * bound_tiles + at_lane - own_tiles,
    )
    flat_cols = remapped.reshape(-1)
    live_grid = jnp.arange(tile_cols.shape[1], dtype=jnp.int32)[None, :] < tile_count[:, None]
    live_tiles = live_grid.reshape(-1)
    flat_tiles = tile_vals.reshape(-1, 128, 128)
    polarity = (2 * excitatory - 1).astype(jnp.float32)
    state = state0
    saved = []
    for moment in range(STEPS):
        rates = jnp.tanh(state)
        signed = (polarity * rates).astype(jnp.bfloat16)
        batch_rows = signed.shape[0]
        gathered_own = lax.all_gather(signed, ROW, axis=1, tiled=True)
        outgoing = jnp.take(signed, chosen, axis=1).reshape(batch_rows, groups, -1)
        incoming = from_each_region(outgoing, me)
        latent = lax.psum(
            jnp.dot(signed, v_factor.T, preferred_element_type=jnp.float32), REGION_ROW
        )
        gathered_border = lax.all_gather(incoming, ROW, axis=1, tiled=True)
        gathered = jnp.concatenate([gathered_own, gathered_border], axis=1)
        synaptic = apply_tiles(gathered, flat_cols, live_tiles, flat_tiles, row_tiles)
        latent_b = latent.astype(jnp.bfloat16)
        lowrank = jnp.dot(latent_b, u_factor, preferred_element_type=jnp.float32)
        saved.append((rates, signed, latent_b))
        state = state + leak * (-state + synaptic + lowrank + drive.astype(jnp.float32))
    grad_u = jnp.zeros((u_factor.shape[0], own_rows), jnp.float32)
    grad_v = jnp.zeros((v_factor.shape[0], own_rows), jnp.float32)
    adjoint = cotangent
    for moment in reversed(range(STEPS)):
        rates, signed, latent_b = saved[moment]
        scaled_b = (leak * adjoint).astype(jnp.bfloat16)
        coeffs = lax.psum(
            jnp.dot(scaled_b, u_factor.T, preferred_element_type=jnp.float32), REGION_ROW
        )
        coeffs_b = coeffs.astype(jnp.bfloat16)
        batch_rows = scaled_b.shape[0]
        spread = jnp.einsum(
            "bri,rjik->brjk",
            scaled_b.reshape(batch_rows, row_tiles, 128),
            tile_vals,
            preferred_element_type=jnp.float32,
        )
        spread = jnp.where(live_grid[None, :, :, None], spread, 0.0)
        columns = jnp.zeros((batch_rows, lanes * per_lane, 128), jnp.float32)
        columns = columns.at[:, flat_cols, :].add(spread.reshape(batch_rows, -1, 128))
        rounded = columns.astype(jnp.bfloat16).astype(jnp.float32)
        own_cols = rounded[:, : lanes * own_tiles].reshape(batch_rows, -1)
        border_cols = rounded[:, lanes * own_tiles :].reshape(batch_rows, -1)
        border = lax.psum_scatter(border_cols, ROW, scatter_dimension=1, tiled=True)
        returned = from_each_region(border.reshape(batch_rows, groups, -1), me)
        own_part = lax.psum_scatter(own_cols, ROW, scatter_dimension=1, tiled=True)
        through = own_part.at[:, chosen].add(returned)
        total_signed = through + jnp.dot(coeffs_b, v_factor, preferred_element_type=jnp.float32)
        grad_u = grad_u + jnp.dot(latent_b.T, scaled_b, preferred_element_type=jnp.float32)
        grad_v = grad_v + jnp.dot(coeffs_b.T, signed, preferred_element_type=jnp.float32)
        adjoint = (1.0 - leak) * adjoint + (1.0 - rates * rates) * polarity * total_signed
    return (state, grad_u, grad_v)


def solution(mesh):
    finer = Mesh(
        mesh.devices.reshape(mesh.shape["region"], 4, 4, 2), ("region", "row_0", "row_1", "row_2")
    )
    in_specs = (
        P(None, REGION_ROW),
        P(None, REGION_ROW),
        P(None, REGION_ROW),
        P(REGION_ROW),
        P(REGION_ROW, None, None, None),
        P(REGION_ROW, None),
        P(REGION_ROW),
        P("region", ROW, None, None),
        P(None, REGION_ROW),
        P(None, REGION_ROW),
    )
    out_specs = (P(None, REGION_ROW), P(None, REGION_ROW), P(None, REGION_ROW))
    return jax.shard_map(local, mesh=finer, in_specs=in_specs, out_specs=out_specs, check_vma=False)
```

profile of v0, /device:TPU:1, one launch (start us, length us, event | category | flops | bytes accessed | tf_op | source)
XLA Modules:
  0.0 1002.2 jit_solution(16985678666152582495)
XLA Ops:
  8.1 1.5 multiply_convert_fusion.4
  12.2 23.3 %all_gather.46 = bf16[8,32,8,16]{1,3,2,0:T(8,128)(2,1)S(1)} all-gather(bf16[1,32,8,16]{1,3,2,0:T(8,128)(2,1)S(1)} %bitcast.256), channel_id=1, replica_groups=mesh['region'=8,'row_0'=4,'row_1'=4,'row_2'=2] {'region'}, dimensions={0}, use_global_device_ids=true | all-gather | bytes 73728 | tf_op jit(solution)/shard_map/all_gather | solution.py:23
  38.0 81.1 %psum.56 = bf16[32,32]{1,0:T(8,128)(2,1)S(1)} all-reduce(f32[32,32]{1,0:T(8,128)S(1)} %fusion.61), channel_id=1, replica_groups=mesh['region'=8,'row_0'=4,'row_1'=4,'row_2'=2] {'region','row_0','row_1'..., use_global_device_ids=true, to_apply=%region_1.3 | all-reduce | flops 1024 | bytes 6144 | tf_op jit(solution)/shard_map/psum | solution.py:71
  119.2 24.4 %all_gather.47 = bf16[32,4096]{1,0:T(8,128)(2,1)S(1)} all-gather(bf16[32,128]{1,0:T(8,128)(2,1)S(1)} %copy.91), channel_id=1, replica_groups=mesh['region'=8,'row_0'=4,'row_1'=4,'row_2'=2] {'row_0','row_1','row_2'}, dimensions={1}, use_global_device_ids=true | all-gather | bytes 270336 | tf_op jit(solution)/shard_map/all_gather | solution.py:74
  143.6 2.5 copy_bitcast_fusion.6
  146.1 2.9 gather_fusion
  149.0 4.1 fusion.18
  153.2 1.5 reduce_sum.36
  155.6 1.7 convolution_select_fusion.2
  157.3 1.8 broadcast.101.clone
  159.1 13.2 %scatter_fusion = f32[32,160,128]{2,0,1:T(8,128)} fusion(f32[32,160,128]{2,0,1:T(8,128)} %broadcast.101.clone, s32[96]{0:T(128)S(1)} %fusion.53, f32[96,32,128]{2,1,0:T(8,128)} %bitcast.243), kind=kCustom, calls=%fused_computation.8 | custom fusion | flops 393216 | bytes 4718976 | tf_op jit(solution)/shard_map/scatter-add | solution.py:100
  172.4 2.0 convert_convert_fusion.2
  174.3 1.5 copy-done.1
  176.7 3.1 copy_bitcast_fusion.2
  181.5 19.1 %all_gather.49 = bf16[8,32,8,16]{1,3,2,0:T(8,128)(2,1)S(1)} all-gather(bf16[1,32,8,16]{1,3,2,0:T(8,128)(2,1)S(1)} %bitcast.257), channel_id=1, replica_groups=mesh['region'=8,'row_0'=4,'row_1'=4,'row_2'=2] {'region'}, dimensions={0}, use_global_device_ids=true | all-gather | bytes 73728 | tf_op jit(solution)/shard_map/all_gather | solution.py:23
  201.4 77.0 %psum.57 = bf16[32,32]{1,0:T(8,128)(2,1)} all-reduce(f32[32,32]{1,0:T(8,128)S(1)} %fusion.62), channel_id=1, replica_groups=mesh['region'=8,'row_0'=4,'row_1'=4,'row_2'=2] {'region','row_0','row_1'..., use_global_device_ids=true, to_apply=%region_3.5 | all-reduce | flops 1024 | bytes 6144 | tf_op jit(solution)/shard_map/psum | solution.py:71
  278.4 24.3 %all_gather.50 = bf16[32,4096]{1,0:T(8,128)(2,1)S(1)} all-gather(bf16[32,128]{1,0:T(8,128)(2,1)} %copy.95), channel_id=1, replica_groups=mesh['region'=8,'row_0'=4,'row_1'=4,'row_2'=2] {'row_0','row_1','row_2'}, dimensions={1}, use_global_device_ids=true | all-gather | bytes 270336 | tf_op jit(solution)/shard_map/all_gather | solution.py:74
  302.8 2.5 copy_bitcast_fusion.5
  305.3 3.0 gather_fusion.1
  308.4 4.2 fusion.16
  312.5 1.5 reduce_sum.37
  317.1 19.2 %all_gather.57 = f32[8,32,8,16]{1,3,2,0:T(8,128)S(1)} all-gather(f32[1,32,8,16]{1,3,2,0:T(8,128)S(1)} %bitcast.249), channel_id=1, replica_groups=mesh['region'=8,'row_0'=4,'row_1'=4,'row_2'=2] {'region'}, dimensions={0}, use_global_device_ids=true | all-gather | bytes 147456 | tf_op jit(solution)/shard_map/all_gather | solution.py:23
  338.7 19.3 %all_gather.52 = bf16[8,32,8,16]{1,3,2,0:T(8,128)(2,1)S(1)} all-gather(bf16[1,32,8,16]{1,3,2,0:T(8,128)(2,1)S(1)} %bitcast.258), channel_id=1, replica_groups=mesh['region'=8,'row_0'=4,'row_1'=4,'row_2'=2] {'region'}, dimensions={0}, use_global_device_ids=true | all-gather | bytes 73728 | tf_op jit(solution)/shard_map/all_gather | solution.py:23
  360.9 83.6 %all-reduce.1 = (bf16[32,32]{1,0:T(8,128)(2,1)}, bf16[32,32]{1,0:T(8,128)(2,1)S(1)}) all-reduce(f32[32,32]{1,0:T(8,128)S(1)} %fusion.63, f32[32,32]{1,0:T(8,128)} %fusion.65), channel_id=1, replica_groups=mesh['region'=8,'row_0'=4,'row_1'=4,'row_2'=2] {'region','row_0','row_1'..., use_global_device_ids=true, to_apply=%region_5.7 | all-reduce | flops 2048 | bytes 12288 | tf_op jit(solution)/shard_map/psum | solution.py:71
  445.1 1.6 convolution_add_fusion.8
  447.7 1.9 scatter_fusion.1
  450.3 24.4 %all_gather.53 = bf16[32,4096]{1,0:T(8,128)(2,1)S(1)} all-gather(bf16[32,128]{1,0:T(8,128)(2,1)} %copy.99), channel_id=1, replica_groups=mesh['region'=8,'row_0'=4,'row_1'=4,'row_2'=2] {'row_0','row_1','row_2'}, dimensions={1}, use_global_device_ids=true | all-gather | bytes 270336 | tf_op jit(solution)/shard_map/all_gather | solution.py:74
  474.7 2.5 copy_bitcast_fusion.4
  477.2 3.0 gather_fusion.2
  480.2 4.1 fusion.14
  484.4 1.5 reduce_sum.38
  487.4 2.3 convolution_select_fusion.1
  489.7 1.8 broadcast.101.clone.1
  491.6 13.2 %scatter_fusion.2 = f32[32,160,128]{2,0,1:T(8,128)} fusion(f32[32,160,128]{2,0,1:T(8,128)} %broadcast.101.clone.1, s32[96]{0:T(128)S(1)} %copy-done.35, f32[96,32,128]{2,1,0:T(8,128)} %bitcast.244), kind=kCustom, calls=%fused_computation.10 | custom fusion | flops 393216 | bytes 4718976 | tf_op jit(solution)/shard_map/scatter-add | solution.py:100
  504.7 2.0 convert_convert_fusion.1
  506.7 1.5 copy-done.2
  509.1 3.1 copy_bitcast_fusion.1
  512.4 73.7 %psum.61 = bf16[32,32]{1,0:T(8,128)(2,1)S(1)} all-reduce(f32[32,32]{1,0:T(8,128)S(1)} %fusion.66), channel_id=1, replica_groups=mesh['region'=8,'row_0'=4,'row_1'=4,'row_2'=2] {'region','row_0','row_1'..., use_global_device_ids=true, to_apply=%region_15.17 | all-reduce | flops 1024 | bytes 6144 | tf_op jit(solution)/shard_map/psum | solution.py:87
  586.2 1.7 reduce-scatter.13.cloned.1.call-done
  588.7 21.2 %all_gather.58 = f32[8,32,8,16]{1,3,2,0:T(8,128)S(1)} all-gather(f32[1,32,8,16]{1,3,2,0:T(8,128)S(1)} %bitcast.250), channel_id=1, replica_groups=mesh['region'=8,'row_0'=4,'row_1'=4,'row_2'=2] {'region'}, dimensions={0}, use_global_device_ids=true | all-gather | bytes 147456 | tf_op jit(solution)/shard_map/all_gather | solution.py:23
  610.5 67.1 %reduce-scatter.11.cloned.1.call-done = f32[32,512]{1,0:T(8,128)} async-done(((f32[32,16384]{1,0:T(8,128)}), f32[32,512]{1,0:T(8,128)}) %reduce-scatter.11.cloned.1.call-update) | async-done | bytes 65552 | tf_op jit(solution)/shard_map/reduce_scatter | solution.py:106
  677.6 1.6 convolution_add_fusion.6
  680.1 1.7 scatter_fusion.3
  683.5 2.3 convolution_select_fusion
  685.8 1.8 broadcast.101
  687.6 13.2 %scatter_fusion.4 = f32[32,160,128]{2,0,1:T(8,128)} fusion(f32[32,160,128]{2,0,1:T(8,128)} %broadcast.101, s32[96]{0:T(128)S(1)} %copy-done.36, f32[96,32,128]{2,1,0:T(8,128)} %bitcast.242), kind=kCustom, calls=%fused_computation.12 | custom fusion | flops 393216 | bytes 4718976 | tf_op jit(solution)/shard_map/scatter-add | solution.py:100
  700.8 2.0 convert_convert_fusion
  702.8 1.5 copy-done.3
  705.2 3.1 copy_bitcast_fusion
  710.0 20.6 %all_gather.55 = bf16[8,32,8,16]{1,3,2,0:T(8,128)(2,1)S(1)} all-gather(bf16[1,32,8,16]{1,3,2,0:T(8,128)(2,1)S(1)} %bitcast.255), channel_id=1, replica_groups=mesh['region'=8,'row_0'=4,'row_1'=4,'row_2'=2] {'region'}, dimensions={0}, use_global_device_ids=true | all-gather | bytes 73728 | tf_op jit(solution)/shard_map/all_gather | solution.py:23
  732.6 31.8 %all_gather.56 = bf16[32,4096]{1,0:T(8,128)(2,1)S(1)} all-gather(bf16[32,128]{1,0:T(8,128)(2,1)} %copy.103), channel_id=1, replica_groups=mesh['region'=8,'row_0'=4,'row_1'=4,'row_2'=2] {'row_0','row_1','row_2'}, dimensions={1}, use_global_device_ids=true | all-gather | bytes 270336 | tf_op jit(solution)/shard_map/all_gather | solution.py:74
  766.8 1.6 convolution_add_fusion.2
  768.4 2.5 copy_bitcast_fusion.3
  770.9 3.0 gather_fusion.3
  774.0 4.1 fusion.12
  778.1 2.1 reduce_sum.39
  780.3 74.4 %psum.62 = bf16[32,32]{1,0:T(8,128)(2,1)S(1)} all-reduce(f32[32,32]{1,0:T(8,128)S(1)} %fusion.67), channel_id=1, replica_groups=mesh['region'=8,'row_0'=4,'row_1'=4,'row_2'=2] {'region','row_0','row_1'..., use_global_device_ids=true, to_apply=%region_20.22 | all-reduce | flops 1024 | bytes 6144 | tf_op jit(solution)/shard_map/psum | solution.py:87
  856.4 19.5 %all_gather.59 = f32[8,32,8,16]{1,3,2,0:T(8,128)S(1)} all-gather(f32[1,32,8,16]{1,3,2,0:T(8,128)S(1)} %bitcast.251), channel_id=1, replica_groups=mesh['region'=8,'row_0'=4,'row_1'=4,'row_2'=2] {'region'}, dimensions={0}, use_global_device_ids=true | all-gather | bytes 147456 | tf_op jit(solution)/shard_map/all_gather | solution.py:23
  876.5 28.5 %reduce-scatter.15.cloned.1.call-done = f32[32,512]{1,0:T(8,128)} async-done(((f32[32,16384]{1,0:T(8,128)}), f32[32,512]{1,0:T(8,128)}) %reduce-scatter.15.cloned.1.call-update) | async-done | bytes 65552 | tf_op jit(solution)/shard_map/reduce_scatter | solution.py:106
  905.0 1.6 convolution_add_fusion.4
  907.6 1.7 scatter_fusion.5
  911.1 77.4 %all-reduce = (bf16[32,32]{1,0:T(8,128)(2,1)S(1)}, bf16[32,32]{1,0:T(8,128)(2,1)S(1)}) all-reduce(f32[32,32]{1,0:T(8,128)} %fusion.64, f32[32,32]{1,0:T(8,128)S(1)} %fusion.68), channel_id=1, replica_groups=mesh['region'=8,'row_0'=4,'row_1'=4,'row_2'=2] {'region','row_0','row_1'..., use_global_device_ids=true, to_apply=%region_7.9 | all-reduce | flops 2048 | bytes 12288 | tf_op jit(solution)/shard_map/psum | solution.py:71
  992.1 1.7 convolution_add_fusion
  993.7 1.6 fusion.2
  (173 shorter events, 43.3 us)
Async XLA Ops:
  7.2 141.8 %copy-start = (bf16[4,24,128,128]{3,2,1,0:T(8,128)(2,1)S(1)}, bf16[4,24,128,128]{3,2,1,0:T(8,128)(2,1)}, u32[]{:S(2)}) copy-start(bf16[4,24,128,128]{3,2,1,0:T(8,128)(2,1)} %param.16) | copy-start | bytes 9437188
  7.2 136.4 %all-gather.5.cloned.1.call-start = ((), (), s32[]{:S(2)}) async-start(), calls=%async_computation.6 | async-start | bytes 1081344 | tf_op jit(solution)/shard_map/all_gather | solution.py:68
  9.6 293.2 %all-gather.7.cloned.1.call-start = ((), (), s32[]{:S(2)}) async-start(), calls=%async_computation.7 | async-start | bytes 1081344 | tf_op jit(solution)/shard_map/all_gather | solution.py:68
  12.1 169.3 %copy-start.31 = (pred[128]{0:T(512)(128)(4,1)}, pred[128]{0:T(512)(128)(4,1)S(1)}, u32[]{:S(2)}) copy-start(pred[128]{0:T(512)(128)(4,1)S(1)} %compare_and_fusion) | copy-start | bytes 388
  37.1 118.5 %copy-start.37 = (pred[4,24]{1,0:T(4,128)(4,1)}, pred[4,24]{1,0:T(4,128)(4,1)S(1)}, u32[]{:S(2)}) copy-start(pred[4,24]{1,0:T(4,128)(4,1)S(1)} %iota_compare_fusion) | copy-start | bytes 292
  37.1 111.8 %copy-start.28 = (pred[96]{0:T(512)(128)(4,1)}, pred[96]{0:T(512)(128)(4,1)S(1)}, u32[]{:S(2)}) copy-start(pred[96]{0:T(512)(128)(4,1)S(1)} %lt.81) | copy-start | bytes 292
  143.5 15.6 %copy-start.34 = (s32[96]{0:T(128)}, s32[96]{0:T(128)S(1)}, u32[]{:S(2)}) copy-start(s32[96]{0:T(128)S(1)} %fusion.53) | copy-start | bytes 1156
  143.5 5.4 copy-start.27
  149.0 5.7 copy-start.4
  149.0 5.7 copy-start.10
  149.0 5.7 copy-start.18
  149.0 6.5 copy-start.21
  155.5 160.8 %reduce-scatter.9.cloned.1.call-start = ((), (), s32[]{:S(2)}) async-start(), calls=%async_computation.11 | async-start | bytes 540672 | tf_op jit(solution)/shard_map/reduce_scatter | solution.py:104
  155.6 1.7 copy-start.13
  174.3 1.5 copy-start.1
  176.7 267.8 %reduce-scatter.7.cloned.1.call-start = ((), (), s32[]{:S(2)}) async-start(), calls=%async_computation.10 | async-start | bytes 2162688 | tf_op jit(solution)/shard_map/reduce_scatter | solution.py:106
  179.8 0.8 copy-start.6
  179.8 21.5 %copy-start.5 = (bf16[32,512]{1,0:T(8,128)(2,1)S(1)}, bf16[32,512]{1,0:T(8,128)(2,1)}, u32[]{:S(2)}) copy-start(bf16[32,512]{1,0:T(8,128)(2,1)} %param.21) | copy-start | bytes 98308
  179.8 294.9 %all-gather.9.cloned.1.call-start = ((), (), s32[]{:S(2)}) async-start(), calls=%async_computation.8 | async-start | bytes 1081344 | tf_op jit(solution)/shard_map/all_gather | solution.py:68
  302.8 5.6 copy-start.29
  308.4 5.7 copy-start.9
  308.4 5.7 copy-start.11
  308.4 5.7 copy-start.23
  308.4 6.6 copy-start.26
  308.4 7.2 copy-start.14
  312.5 26.0 %copy-start.32 = (pred[128]{0:T(512)(128)(4,1)S(1)}, pred[128]{0:T(512)(128)(4,1)}, u32[]{:S(2)}) copy-start(pred[128]{0:T(512)(128)(4,1)} %copy-done.31) | copy-start | bytes 388
  314.9 273.0 %reduce-scatter.13.cloned.1.call-start = ((), (), s32[]{:S(2)}) async-start(), calls=%async_computation.13 | async-start | bytes 540672 | tf_op jit(solution)/shard_map/reduce_scatter | solution.py:104
  444.5 0.6 copy-start.25
  480.2 5.6 copy-start.12
  480.2 5.6 copy-start.20
  480.2 5.7 copy-start.22
  487.4 24.9 %copy-start.15 = (bf16[32,512]{1,0:T(8,128)(2,1)}, bf16[32,512]{1,0:T(8,128)(2,1)S(1)}, u32[]{:S(2)}) copy-start(bf16[32,512]{1,0:T(8,128)(2,1)S(1)} %get-tuple-element.8) | copy-start | bytes 98308
  489.7 1.9 copy-start.35
  506.7 1.5 copy-start.2
  509.1 168.5 %reduce-scatter.11.cloned.1.call-start = ((), (), s32[]{:S(2)}) async-start(), calls=%async_computation.12 | async-start | bytes 2162688 | tf_op jit(solution)/shard_map/reduce_scatter | solution.py:106
  512.2 256.2 %all-gather.11.cloned.1.call-start = ((), (), s32[]{:S(2)}) async-start(), calls=%async_computation.9 | async-start | bytes 1081344 | tf_op jit(solution)/shard_map/all_gather | solution.py:68
  586.1 91.5 %copy-start.24 = (bf16[32,32]{1,0:T(8,128)(2,1)}, bf16[32,32]{1,0:T(8,128)(2,1)S(1)}, u32[]{:S(2)}) copy-start(bf16[32,32]{1,0:T(8,128)(2,1)S(1)} %psum.61) | copy-start | bytes 6148
  586.2 269.4 %reduce-scatter.17.cloned.1.call-start = ((), (), s32[]{:S(2)}) async-start(), calls=%async_computation.15 | async-start | bytes 540672 | tf_op jit(solution)/shard_map/reduce_scatter | solution.py:104
  683.5 2.3 copy-start.16
  685.8 1.9 copy-start.36
  702.8 1.5 copy-start.3
  705.2 199.8 %reduce-scatter.15.cloned.1.call-start = ((), (), s32[]{:S(2)}) async-start(), calls=%async_computation.14 | async-start | bytes 2162688 | tf_op jit(solution)/shard_map/reduce_scatter | solution.py:106
  708.3 0.8 copy-start.8
  708.3 1.6 copy-start.33
  768.4 5.5 copy-start.30
  773.9 6.3 copy-start.17
  773.9 80.8 %copy-start.7 = (bf16[32,512]{1,0:T(8,128)(2,1)S(1)}, bf16[32,512]{1,0:T(8,128)(2,1)}, u32[]{:S(2)}) copy-start(bf16[32,512]{1,0:T(8,128)(2,1)} %get-tuple-element.11) | copy-start | bytes 98308
  774.0 80.8 %copy-start.19 = (f32[32,512]{1,0:T(8,128)S(1)}, f32[32,512]{1,0:T(8,128)}, u32[]{:S(2)}) copy-start(f32[32,512]{1,0:T(8,128)} %convolution_add_fusion.2) | copy-start | bytes 196612
  778.1 129.5 %copy-start.38 = (s32[128]{0:T(128)S(1)}, s32[128]{0:T(128)}, u32[]{:S(2)}) copy-start(s32[128]{0:T(128)} %fusion.54) | copy-start | bytes 1540
Sparse Core Ops, SparseCore 0:
  10.5 52.4 all-gather.4
  155.6 44.2 all-gather.6
  203.6 81.8 reduce-scatter.8
  289.2 85.9 reduce-scatter.6
  377.6 49.4 all-gather.8
  509.2 78.6 reduce-scatter.12
  591.7 85.8 reduce-scatter.10
  680.1 49.4 all-gather.10
  733.3 82.0 reduce-scatter.16
  819.1 85.8 reduce-scatter.14
where the time goes:
time: 1010 us; the launch traced here: 1000 us
  blocking collectives  714 us (71%)
  waiting for transfers between devices  97.5 us (10%)
  other arithmetic  74.2 us (7%)
  local copies, waits for them, and re-layouts  56 us (6%)
  matrix products  45.3 us (4%)
  between operations  14.6 us (1%)
    psum x4, blocking collectives, local(): lax.psum(jnp.dot(signed, v_factor.T, preferred_element_type=jnp.float32),...  319 us
    psum x2, blocking collectives, local(): lax.psum(jnp.dot(scaled_b, u_factor.T, preferred_element_type=jnp.float32...  148 us
    all_gather x7, blocking collectives, from_each_region(): everyone = lax.all_gather(x, 'region', axis=0, tiled=False)  142 us
    all_gather x4, blocking collectives, local(): gathered_border = lax.all_gather(incoming, ROW, axis=1, tiled=True)  105 us
    reduce_scatter x3, waiting for transfers between devices, local(): own_part = lax.psum_scatter(own_cols, ROW, scatter_dimension=1, tiled=True)  95.6 us
    scatter-add x3, other arithmetic, local(): columns.at[:, flat_cols, :].add(spread.reshape(batch_rows, -1, 128))  39.6 us
  transfers between devices with their start and end apart: 10, of which 3 were waited for; matrix products, arithmetic and copies ran while one was open for 11% of the time, Pallas kernels for 0%

commit v1 on v0

--- a/solution.py
+++ b/solution.py
@@ -71,7 +71,9 @@
         latent = lax.psum(
             jnp.dot(signed, v_factor.T, preferred_element_type=jnp.float32), REGION_ROW
         )
-        gathered_border = lax.all_gather(incoming, ROW, axis=1, tiled=True)
+        gathered_border = jnp.concatenate(
+            lax.all_to_all(jnp.stack([incoming] * lax.axis_size(ROW)), ROW, 0, 0), axis=1
+        )
         gathered = jnp.concatenate([gathered_own, gathered_border], axis=1)
         synaptic = apply_tiles(gathered, flat_cols, live_tiles, flat_tiles, row_tiles)
         latent_b = latent.astype(jnp.bfloat16)

time: 1010 us -> 965 us (0.955)
  blocking collectives: 714 us -> 597 us
  starting transfers between devices: 0.41 us -> 55.3 us
  waiting for transfers between devices: 97.5 us -> 120 us
    all_gather x4 -> x0, blocking collectives: 105 us -> none  [local(): gathered_border = lax.all_gather(incoming, ROW, axis=1, tiled=True)]
    all_to_all x0 -> x4, starting transfers between devices: none -> 54.9 us  [local(): lax.all_to_all(jnp.stack([incoming] * lax.axis_size(ROW)), ROW, 0, 0)]
    reduce_scatter x3, waiting for transfers between devices: 95.6 us -> 110 us  [local(): own_part = lax.psum_scatter(own_cols, ROW, scatter_dimension=1, tiled=True)]
    psum x4, blocking collectives: 319 us -> 307 us  [local(): lax.psum(jnp.dot(signed, v_factor.T, preferred_element_type=jnp.float32),...]
  transfers between devices with their start and end apart: 10 -> 14, of which waited for: 3 -> 4; matrix products, arithmetic and copies ran while one was open for 11% -> 11% of each run, Pallas kernels for 0% -> 0%
where the time goes in v1:
time: 965 us; the launch traced here: 962 us
  blocking collectives  597 us (62%)
  waiting for transfers between devices  120 us (12%)
  other arithmetic  74 us (8%)
  local copies, waits for them, and re-layouts  58.9 us (6%)
  starting transfers between devices  55.3 us (6%)
  matrix products  42.3 us (4%)
  between operations  14.8 us (2%)
    psum x4, blocking collectives, local(): lax.psum(jnp.dot(signed, v_factor.T, preferred_element_type=jnp.float32),...  307 us
    psum x2, blocking collectives, local(): lax.psum(jnp.dot(scaled_b, u_factor.T, preferred_element_type=jnp.float32...  148 us
    all_gather x7, blocking collectives, from_each_region(): everyone = lax.all_gather(x, 'region', axis=0, tiled=False)  142 us
    reduce_scatter x3, waiting for transfers between devices, local(): own_part = lax.psum_scatter(own_cols, ROW, scatter_dimension=1, tiled=True)  110 us
    all_to_all x4, starting transfers between devices, local(): lax.all_to_all(jnp.stack([incoming] * lax.axis_size(ROW)), ROW, 0, 0)  54.9 us
    scatter-add x3, other arithmetic, local(): columns.at[:, flat_cols, :].add(spread.reshape(batch_rows, -1, 128))  39.6 us
  transfers between devices with their start and end apart: 14, of which 4 were waited for; matrix products, arithmetic and copies ran while one was open for 11% of the time, Pallas kernels for 0%

profile of v1, /device:TPU:1, one launch (start us, length us, event | category | flops | bytes accessed | tf_op | source)
XLA Modules:
  0.0 962.0 jit_solution(1568649331610203075)
XLA Ops:
  8.1 1.5 multiply_convert_fusion.4
  12.1 23.3 %all_gather.34 = bf16[8,32,8,16]{1,3,2,0:T(8,128)(2,1)S(1)} all-gather(bf16[1,32,8,16]{1,3,2,0:T(8,128)(2,1)S(1)} %bitcast.280), channel_id=1, replica_groups=mesh['region'=8,'row_0'=4,'row_1'=4,'row_2'=2] {'region'}, dimensions={0}, use_global_device_ids=true | all-gather | bytes 73728 | tf_op jit(solution)/shard_map/all_gather | solution.py:23
  36.2 13.9 %all-to-all-start = ((bf16[32,32,128]{2,1,0:T(8,128)(2,1)}), bf16[32,32,128]{2,1,0:T(8,128)(2,1)}, u32[]{:S(2)}, u32[]{:S(2)}) async-start(bf16[32,32,128]{2,1,0:T(8,128)(2,1)} %stack.12), calls=%async_computation | async-start | bytes 524288 | tf_op jit(solution)/shard_map/all_to_all | solution.py:75
  52.7 76.7 %psum.56 = bf16[32,32]{1,0:T(8,128)(2,1)S(1)} all-reduce(f32[32,32]{1,0:T(8,128)S(1)} %fusion.61), channel_id=1, replica_groups=mesh['region'=8,'row_0'=4,'row_1'=4,'row_2'=2] {'region','row_0','row_1'..., use_global_device_ids=true, to_apply=%region_1.3 | all-reduce | flops 1024 | bytes 6144 | tf_op jit(solution)/shard_map/psum | solution.py:71
  130.4 2.5 copy_bitcast_fusion.6
  133.0 2.9 gather_fusion
  135.9 4.1 fusion.18
  140.0 1.5 reduce_sum.36
  142.5 1.7 convolution_select_fusion.2
  144.2 1.8 broadcast.105.clone
  146.0 13.2 %scatter_fusion = f32[32,160,128]{2,0,1:T(8,128)} fusion(f32[32,160,128]{2,0,1:T(8,128)} %broadcast.105.clone, s32[96]{0:T(128)S(1)} %fusion.53, f32[96,32,128]{2,1,0:T(8,128)} %bitcast.267), kind=kCustom, calls=%fused_computation.8 | custom fusion | flops 393216 | bytes 4718976 | tf_op jit(solution)/shard_map/scatter-add | solution.py:102
  159.2 2.0 convert_convert_fusion.2
  161.2 1.5 copy-done.1
  163.6 3.1 copy_bitcast_fusion.2
  168.4 19.1 %all_gather.36 = bf16[8,32,8,16]{1,3,2,0:T(8,128)(2,1)S(1)} all-gather(bf16[1,32,8,16]{1,3,2,0:T(8,128)(2,1)S(1)} %bitcast.281), channel_id=1, replica_groups=mesh['region'=8,'row_0'=4,'row_1'=4,'row_2'=2] {'region'}, dimensions={0}, use_global_device_ids=true | all-gather | bytes 73728 | tf_op jit(solution)/shard_map/all_gather | solution.py:23
  188.4 11.0 %all-to-all-start.1 = ((bf16[32,32,128]{2,1,0:T(8,128)(2,1)}), bf16[32,32,128]{2,1,0:T(8,128)(2,1)}, u32[]{:S(2)}, u32[]{:S(2)}) async-start(bf16[32,32,128]{2,1,0:T(8,128)(2,1)} %stack.13), calls=%async_computation.1 | async-start | bytes 524288 | tf_op jit(solution)/shard_map/all_to_all | solution.py:75
  200.9 76.8 %psum.57 = bf16[32,32]{1,0:T(8,128)(2,1)} all-reduce(f32[32,32]{1,0:T(8,128)S(1)} %fusion.62), channel_id=1, replica_groups=mesh['region'=8,'row_0'=4,'row_1'=4,'row_2'=2] {'region','row_0','row_1'..., use_global_device_ids=true, to_apply=%region_3.5 | all-reduce | flops 1024 | bytes 6144 | tf_op jit(solution)/shard_map/psum | solution.py:71
  278.6 2.5 copy_bitcast_fusion.5
  281.2 3.0 gather_fusion.1
  284.2 4.1 fusion.16
  288.3 1.5 reduce_sum.37
  292.1 19.3 %all_gather.41 = f32[8,32,8,16]{1,3,2,0:T(8,128)S(1)} all-gather(f32[1,32,8,16]{1,3,2,0:T(8,128)S(1)} %bitcast.273), channel_id=1, replica_groups=mesh['region'=8,'row_0'=4,'row_1'=4,'row_2'=2] {'region'}, dimensions={0}, use_global_device_ids=true | all-gather | bytes 147456 | tf_op jit(solution)/shard_map/all_gather | solution.py:23
  313.7 18.9 %all_gather.38 = bf16[8,32,8,16]{1,3,2,0:T(8,128)(2,1)S(1)} all-gather(bf16[1,32,8,16]{1,3,2,0:T(8,128)(2,1)S(1)} %bitcast.282), channel_id=1, replica_groups=mesh['region'=8,'row_0'=4,'row_1'=4,'row_2'=2] {'region'}, dimensions={0}, use_global_device_ids=true | all-gather | bytes 73728 | tf_op jit(solution)/shard_map/all_gather | solution.py:23
  333.4 16.9 %all-to-all-start.2 = ((bf16[32,32,128]{2,1,0:T(8,128)(2,1)}), bf16[32,32,128]{2,1,0:T(8,128)(2,1)}, u32[]{:S(2)}, u32[]{:S(2)}) async-start(bf16[32,32,128]{2,1,0:T(8,128)(2,1)} %stack.14), calls=%async_computation.2 | async-start | bytes 524288 | tf_op jit(solution)/shard_map/all_to_all | solution.py:75
  350.5 76.5 %all-reduce.1 = (bf16[32,32]{1,0:T(8,128)(2,1)}, bf16[32,32]{1,0:T(8,128)(2,1)S(1)}) all-reduce(f32[32,32]{1,0:T(8,128)S(1)} %fusion.63, f32[32,32]{1,0:T(8,128)S(1)} %copy-done.27), channel_id=1, replica_groups=mesh['region'=8,'row_0'=4,'row_1'=4,'row_2'=2] {'region','row_0','row_1'..., use_global_device_ids=true, to_apply=%region_5.7 | all-reduce | flops 2048 | bytes 12288 | tf_op jit(solution)/shard_map/psum | solution.py:71
  427.7 1.6 convolution_add_fusion.8
  430.2 1.7 scatter_fusion.1
  433.6 2.5 copy_bitcast_fusion.4
  436.2 3.0 gather_fusion.2
  439.2 4.1 fusion.14
  443.3 1.5 reduce_sum.38
  444.9 1.5 fusion.60
  446.4 2.3 convolution_select_fusion.1
  448.7 1.8 broadcast.105.clone.1
  450.5 13.2 %scatter_fusion.2 = f32[32,160,128]{2,0,1:T(8,128)} fusion(f32[32,160,128]{2,0,1:T(8,128)} %broadcast.105.clone.1, s32[96]{0:T(128)S(1)} %copy-done.40, f32[96,32,128]{2,1,0:T(8,128)} %bitcast.268), kind=kCustom, calls=%fused_computation.10 | custom fusion | flops 393216 | bytes 4718976 | tf_op jit(solution)/shard_map/scatter-add | solution.py:102
  463.7 2.0 convert_convert_fusion.1
  465.7 1.5 copy-done.2
  468.1 3.1 copy_bitcast_fusion.1
  471.4 74.2 %psum.61 = bf16[32,32]{1,0:T(8,128)(2,1)S(1)} all-reduce(f32[32,32]{1,0:T(8,128)S(1)} %fusion.66), channel_id=1, replica_groups=mesh['region'=8,'row_0'=4,'row_1'=4,'row_2'=2] {'region','row_0','row_1'..., use_global_device_ids=true, to_apply=%region_15.17 | all-reduce | flops 1024 | bytes 6144 | tf_op jit(solution)/shard_map/psum | solution.py:89
  545.7 1.9 reduce-scatter.13.cloned.1.call-done
  548.4 21.2 %all_gather.42 = f32[8,32,8,16]{1,3,2,0:T(8,128)S(1)} all-gather(f32[1,32,8,16]{1,3,2,0:T(8,128)S(1)} %bitcast.274), channel_id=1, replica_groups=mesh['region'=8,'row_0'=4,'row_1'=4,'row_2'=2] {'region'}, dimensions={0}, use_global_device_ids=true | all-gather | bytes 147456 | tf_op jit(solution)/shard_map/all_gather | solution.py:23
  570.3 67.0 %reduce-scatter.11.cloned.1.call-done = f32[32,512]{1,0:T(8,128)} async-done(((f32[32,16384]{1,0:T(8,128)}), f32[32,512]{1,0:T(8,128)}) %reduce-scatter.11.cloned.1.call-update) | async-done | bytes 65552 | tf_op jit(solution)/shard_map/reduce_scatter | solution.py:108
  637.3 1.6 convolution_add_fusion.6
  639.8 1.7 scatter_fusion.3
  643.2 2.3 convolution_select_fusion
  645.5 1.8 broadcast.105
  647.3 13.2 %scatter_fusion.4 = f32[32,160,128]{2,0,1:T(8,128)} fusion(f32[32,160,128]{2,0,1:T(8,128)} %broadcast.105, s32[96]{0:T(128)S(1)} %copy-done.41, f32[96,32,128]{2,1,0:T(8,128)} %bitcast.266), kind=kCustom, calls=%fused_computation.12 | custom fusion | flops 393216 | bytes 4718976 | tf_op jit(solution)/shard_map/scatter-add | solution.py:102
  660.5 2.0 convert_convert_fusion
  664.9 3.1 copy_bitcast_fusion
  669.7 20.5 %all_gather.40 = bf16[8,32,8,16]{1,3,2,0:T(8,128)(2,1)S(1)} all-gather(bf16[1,32,8,16]{1,3,2,0:T(8,128)(2,1)S(1)} %bitcast.279), channel_id=1, replica_groups=mesh['region'=8,'row_0'=4,'row_1'=4,'row_2'=2] {'region'}, dimensions={0}, use_global_device_ids=true | all-gather | bytes 73728 | tf_op jit(solution)/shard_map/all_gather | solution.py:23
  691.0 13.1 %all-to-all-start.3 = ((bf16[32,32,128]{2,1,0:T(8,128)(2,1)}), bf16[32,32,128]{2,1,0:T(8,128)(2,1)}, u32[]{:S(2)}, u32[]{:S(2)}) async-start(bf16[32,32,128]{2,1,0:T(8,128)(2,1)} %stack.15), calls=%async_computation.3 | async-start | bytes 524288 | tf_op jit(solution)/shard_map/all_to_all | solution.py:75
  705.9 7.2 all-to-all-done.3
  714.1 2.5 copy_bitcast_fusion.3
  716.7 3.0 gather_fusion.3
  719.7 4.1 fusion.12
  723.8 2.2 reduce_sum.39
  726.1 73.8 %psum.62 = bf16[32,32]{1,0:T(8,128)(2,1)S(1)} all-reduce(f32[32,32]{1,0:T(8,128)S(1)} %fusion.67), channel_id=1, replica_groups=mesh['region'=8,'row_0'=4,'row_1'=4,'row_2'=2] {'region','row_0','row_1'..., use_global_device_ids=true, to_apply=%region_20.22 | all-reduce | flops 1024 | bytes 6144 | tf_op jit(solution)/shard_map/psum | solution.py:89
  801.6 19.4 %all_gather.43 = f32[8,32,8,16]{1,3,2,0:T(8,128)S(1)} all-gather(f32[1,32,8,16]{1,3,2,0:T(8,128)S(1)} %bitcast.275), channel_id=1, replica_groups=mesh['region'=8,'row_0'=4,'row_1'=4,'row_2'=2] {'region'}, dimensions={0}, use_global_device_ids=true | all-gather | bytes 147456 | tf_op jit(solution)/shard_map/all_gather | solution.py:23
  821.6 43.2 %reduce-scatter.15.cloned.1.call-done = f32[32,512]{1,0:T(8,128)} async-done(((f32[32,16384]{1,0:T(8,128)}), f32[32,512]{1,0:T(8,128)}) %reduce-scatter.15.cloned.1.call-update) | async-done | bytes 65552 | tf_op jit(solution)/shard_map/reduce_scatter | solution.py:108
  864.7 1.6 convolution_add_fusion.4
  867.3 1.7 scatter_fusion.5
  870.8 77.4 %all-reduce = (bf16[32,32]{1,0:T(8,128)(2,1)S(1)}, bf16[32,32]{1,0:T(8,128)(2,1)S(1)}) all-reduce(f32[32,32]{1,0:T(8,128)} %fusion.64, f32[32,32]{1,0:T(8,128)S(1)} %fusion.68), channel_id=1, replica_groups=mesh['region'=8,'row_0'=4,'row_1'=4,'row_2'=2] {'region','row_0','row_1'..., use_global_device_ids=true, to_apply=%region_7.9 | all-reduce | flops 2048 | bytes 12288 | tf_op jit(solution)/shard_map/psum | solution.py:71
  951.8 1.7 convolution_add_fusion
  953.5 1.6 fusion.2
  (197 shorter events, 44.9 us)
Async XLA Ops:
  7.2 128.7 %copy-start = (bf16[4,24,128,128]{3,2,1,0:T(8,128)(2,1)S(1)}, bf16[4,24,128,128]{3,2,1,0:T(8,128)(2,1)}, u32[]{:S(2)}) copy-start(bf16[4,24,128,128]{3,2,1,0:T(8,128)(2,1)} %param.16) | copy-start | bytes 9437188
  7.2 123.2 %all-gather.5.cloned.1.call-start = ((), (), s32[]{:S(2)}) async-start(), calls=%async_computation.10 | async-start | bytes 1081344 | tf_op jit(solution)/shard_map/all_gather | solution.py:68
  11.3 40.5 %copy-start.32 = (pred[128]{0:T(512)(128)(4,1)}, pred[128]{0:T(512)(128)(4,1)S(1)}, u32[]{:S(2)}) copy-start(pred[128]{0:T(512)(128)(4,1)S(1)} %compare_and_fusion) | copy-start | bytes 388
  36.2 93.2 %all-to-all-start = ((bf16[32,32,128]{2,1,0:T(8,128)(2,1)}), bf16[32,32,128]{2,1,0:T(8,128)(2,1)}, u32[]{:S(2)}, u32[]{:S(2)}) async-start(bf16[32,32,128]{2,1,0:T(8,128)(2,1)} %stack.12), calls=%async_computation | async-start | bytes 524288 | tf_op jit(solution)/shard_map/all_to_all | solution.py:75
  50.2 228.4 %all-gather.7.cloned.1.call-start = ((), (), s32[]{:S(2)}) async-start(), calls=%async_computation.11 | async-start | bytes 1081344 | tf_op jit(solution)/shard_map/all_gather | solution.py:68
  51.7 90.7 %copy-start.42 = (pred[4,24]{1,0:T(4,128)(4,1)}, pred[4,24]{1,0:T(4,128)(4,1)S(1)}, u32[]{:S(2)}) copy-start(pred[4,24]{1,0:T(4,128)(4,1)S(1)} %iota_compare_fusion) | copy-start | bytes 292
  51.8 84.0 %copy-start.36 = (pred[96]{0:T(512)(128)(4,1)}, pred[96]{0:T(512)(128)(4,1)S(1)}, u32[]{:S(2)}) copy-start(pred[96]{0:T(512)(128)(4,1)S(1)} %lt.81) | copy-start | bytes 292
  129.4 16.6 %copy-start.39 = (s32[96]{0:T(128)}, s32[96]{0:T(128)S(1)}, u32[]{:S(2)}) copy-start(s32[96]{0:T(128)S(1)} %fusion.53) | copy-start | bytes 1156
  129.4 6.4 copy-start.31
  135.9 5.7 copy-start.4
  135.9 5.7 copy-start.12
  135.9 5.7 copy-start.19
  135.9 6.5 copy-start.22
  142.4 148.9 %reduce-scatter.9.cloned.1.call-start = ((), (), s32[]{:S(2)}) async-start(), calls=%async_computation.15 | async-start | bytes 540672 | tf_op jit(solution)/shard_map/reduce_scatter | solution.py:106
  142.4 57.0 %copy-start.15 = (bf16[32,512]{1,0:T(8,128)(2,1)}, bf16[32,512]{1,0:T(8,128)(2,1)S(1)}, u32[]{:S(2)}) copy-start(bf16[32,512]{1,0:T(8,128)(2,1)S(1)} %multiply_convert_fusion.5) | copy-start | bytes 98308
  161.2 1.5 copy-start.1
  163.6 263.5 %reduce-scatter.7.cloned.1.call-start = ((), (), s32[]{:S(2)}) async-start(), calls=%async_computation.14 | async-start | bytes 2162688 | tf_op jit(solution)/shard_map/reduce_scatter | solution.py:108
  166.7 0.8 copy-start.6
  166.7 1.6 copy-start.33
  166.7 33.4 %copy-start.30 = (s32[1,1,8,16]{3,2,1,0:T(8,128)S(1)}, s32[1,1,8,16]{3,2,1,0:T(8,128)}, u32[]{:S(2)}) copy-start(s32[1,1,8,16]{3,2,1,0:T(8,128)} %param.19) | copy-start | bytes 1540
  166.7 34.0 %copy-start.5 = (bf16[32,512]{1,0:T(8,128)(2,1)S(1)}, bf16[32,512]{1,0:T(8,128)(2,1)}, u32[]{:S(2)}) copy-start(bf16[32,512]{1,0:T(8,128)(2,1)} %param.21) | copy-start | bytes 98308
  188.4 89.2 %all-to-all-start.1 = ((bf16[32,32,128]{2,1,0:T(8,128)(2,1)}), bf16[32,32,128]{2,1,0:T(8,128)(2,1)}, u32[]{:S(2)}, u32[]{:S(2)}) async-start(bf16[32,32,128]{2,1,0:T(8,128)(2,1)} %stack.13), calls=%async_computation.1 | async-start | bytes 524288 | tf_op jit(solution)/shard_map/all_to_all | solution.py:75
  199.3 234.3 %all-gather.9.cloned.1.call-start = ((), (), s32[]{:S(2)}) async-start(), calls=%async_computation.12 | async-start | bytes 1081344 | tf_op jit(solution)/shard_map/all_gather | solution.py:68
  278.6 5.6 copy-start.37
  284.2 5.7 copy-start.11
  284.2 5.7 copy-start.13
  284.2 5.7 copy-start.24
  284.2 6.5 copy-start.44
  288.3 25.3 %copy-start.34 = (pred[128]{0:T(512)(128)(4,1)S(1)}, pred[128]{0:T(512)(128)(4,1)}, u32[]{:S(2)}) copy-start(pred[128]{0:T(512)(128)(4,1)} %copy-done.32) | copy-start | bytes 388
  288.3 62.2 %copy-start.27 = (f32[32,32]{1,0:T(8,128)S(1)}, f32[32,32]{1,0:T(8,128)}, u32[]{:S(2)}) copy-start(f32[32,32]{1,0:T(8,128)} %fusion.65) | copy-start | bytes 12292
  290.7 59.7 %copy-start.8 = (bf16[32,512]{1,0:T(8,128)(2,1)S(1)}, bf16[32,512]{1,0:T(8,128)(2,1)}, u32[]{:S(2)}) copy-start(bf16[32,512]{1,0:T(8,128)(2,1)} %get-tuple-element.13) | copy-start | bytes 98308
  333.4 99.2 %all-to-all-start.2 = ((bf16[32,32,128]{2,1,0:T(8,128)(2,1)}), bf16[32,32,128]{2,1,0:T(8,128)(2,1)}, u32[]{:S(2)}, u32[]{:S(2)}) async-start(bf16[32,32,128]{2,1,0:T(8,128)(2,1)} %stack.14), calls=%async_computation.2 | async-start | bytes 524288 | tf_op jit(solution)/shard_map/all_to_all | solution.py:75
  350.3 197.2 %reduce-scatter.13.cloned.1.call-start = ((), (), s32[]{:S(2)}) async-start(), calls=%async_computation.17 | async-start | bytes 540672 | tf_op jit(solution)/shard_map/reduce_scatter | solution.py:106
  427.1 0.6 copy-start.28
  439.2 5.7 copy-start.14
  439.2 5.7 copy-start.21
  439.2 5.7 copy-start.23
  446.4 24.9 %copy-start.16 = (bf16[32,512]{1,0:T(8,128)(2,1)}, bf16[32,512]{1,0:T(8,128)(2,1)S(1)}, u32[]{:S(2)}) copy-start(bf16[32,512]{1,0:T(8,128)(2,1)S(1)} %get-tuple-element.8) | copy-start | bytes 98308
  448.7 1.8 copy-start.40
  465.7 1.5 copy-start.2
  468.1 169.2 %reduce-scatter.11.cloned.1.call-start = ((), (), s32[]{:S(2)}) async-start(), calls=%async_computation.16 | async-start | bytes 2162688 | tf_op jit(solution)/shard_map/reduce_scatter | solution.py:108
  471.2 242.9 %all-gather.11.cloned.1.call-start = ((), (), s32[]{:S(2)}) async-start(), calls=%async_computation.13 | async-start | bytes 1081344 | tf_op jit(solution)/shard_map/all_gather | solution.py:68
  545.6 91.7 %copy-start.25 = (bf16[32,32]{1,0:T(8,128)(2,1)}, bf16[32,32]{1,0:T(8,128)(2,1)S(1)}, u32[]{:S(2)}) copy-start(bf16[32,32]{1,0:T(8,128)(2,1)S(1)} %psum.61) | copy-start | bytes 6148
  545.6 255.1 %reduce-scatter.17.cloned.1.call-start = ((), (), s32[]{:S(2)}) async-start(), calls=%async_computation.19 | async-start | bytes 540672 | tf_op jit(solution)/shard_map/reduce_scatter | solution.py:106
  643.1 2.3 copy-start.17
  645.5 1.8 copy-start.41
  662.5 1.5 copy-start.3
  664.9 199.9 %reduce-scatter.15.cloned.1.call-start = ((), (), s32[]{:S(2)}) async-start(), calls=%async_computation.18 | async-start | bytes 2162688 | tf_op jit(solution)/shard_map/reduce_scatter | solution.py:108
  668.0 0.8 copy-start.10
  668.0 1.6 copy-start.35
  668.0 36.1 %copy-start.29 = (bf16[32,32]{1,0:T(8,128)(2,1)S(1)}, bf16[32,32]{1,0:T(8,128)(2,1)}, u32[]{:S(2)}) copy-start(bf16[32,32]{1,0:T(8,128)(2,1)} %copy-done.28) | copy-start | bytes 6148
  668.0 37.0 %copy-start.9 = (bf16[32,512]{1,0:T(8,128)(2,1)S(1)}, bf16[32,512]{1,0:T(8,128)(2,1)}, u32[]{:S(2)}) copy-start(bf16[32,512]{1,0:T(8,128)(2,1)} %get-tuple-element.13) | copy-start | bytes 98308
  668.0 37.0 %copy-start.26 = (bf16[32,32]{1,0:T(8,128)(2,1)S(1)}, bf16[32,32]{1,0:T(8,128)(2,1)}, u32[]{:S(2)}) copy-start(bf16[32,32]{1,0:T(8,128)(2,1)} %copy-done.25) | copy-start | bytes 6148
  691.0 22.1 %all-to-all-start.3 = ((bf16[32,32,128]{2,1,0:T(8,128)(2,1)}), bf16[32,32,128]{2,1,0:T(8,128)(2,1)}, u32[]{:S(2)}, u32[]{:S(2)}) async-start(bf16[32,32,128]{2,1,0:T(8,128)(2,1)} %stack.15), calls=%async_computation.3 | async-start | bytes 524288 | tf_op jit(solution)/shard_map/all_to_all | solution.py:75
  714.1 5.6 copy-start.38
  719.7 6.3 copy-start.18
  719.7 80.3 %copy-start.7 = (bf16[32,512]{1,0:T(8,128)(2,1)S(1)}, bf16[32,512]{1,0:T(8,128)(2,1)}, u32[]{:S(2)}) copy-start(bf16[32,512]{1,0:T(8,128)(2,1)} %get-tuple-element.11) | copy-start | bytes 98308
  719.7 80.3 %copy-start.20 = (f32[32,512]{1,0:T(8,128)S(1)}, f32[32,512]{1,0:T(8,128)}, u32[]{:S(2)}) copy-start(f32[32,512]{1,0:T(8,128)} %convolution_add_fusion.2) | copy-start | bytes 196612
  723.8 143.5 %copy-start.43 = (s32[128]{0:T(128)S(1)}, s32[128]{0:T(128)}, u32[]{:S(2)}) copy-start(s32[128]{0:T(128)} %fusion.54) | copy-start | bytes 1540
Sparse Core Ops, SparseCore 0:
  10.5 53.6 all-gather.4
  142.5 43.7 all-gather.6
  190.0 81.9 reduce-scatter.8
  275.7 86.3 reduce-scatter.6
  364.4 48.9 all-gather.8
  468.2 79.3 reduce-scatter.12
  551.4 85.8 reduce-scatter.10
  639.7 49.4 all-gather.10
  692.9 82.0 reduce-scatter.16
  778.7 85.9 reduce-scatter.14
